TPU v7x, 128 devices: a whole 4x4x4 slice. The times are simulated.
128 devices in a mesh: dp: 4 (over z_hi, core), mp: 32 (over x, y, z_lo).
Axes of the slice: x: 4, y: 4, z: 4 (z_hi: 2, z_lo: 2; z = z_hi * 2 + z_lo), core: 2. Of those that a mesh axis runs over, the one named last changes fastest.
Arguments:
- residual_input: bfloat16 [2048, 4608], P(('dp', 'mp')), may hold values from -6 to 6
- before_attention_gain: float32 [4608], replicated, may hold values from 0.25 to 1.75
- after_attention_gain: float32 [4608], replicated, may hold values from 0.25 to 1.75
- before_feedforward_gain: float32 [4608], replicated, may hold values from 0.25 to 1.75
- after_feedforward_gain: float32 [4608], replicated, may hold values from 0.25 to 1.75
- query_weight: bfloat16 [4608, 4096], P(None, 'mp'), may hold values from -0.09375 to 0.09375
- key_value_weight: bfloat16 [4608, 2, 32, 128], P(None, None, 'mp'), as said below
- output_weight: bfloat16 [4096, 4608], P('mp'), may hold values from -0.09375 to 0.09375
- gate_matrix: bfloat16 [4608, 20480], P(None, 'mp'), may hold values from -0.09375 to 0.09375
- up_matrix: bfloat16 [4608, 20480], P(None, 'mp'), may hold values from -0.09375 to 0.09375
- down_matrix: bfloat16 [20480, 4608], P('mp'), may hold values from -0.0390625 to 0.0390625
- key_value_cache: bfloat16 [256, 2, 32, 16, 128], P('dp', None, 'mp'), as said below
- projected_lowrank_left: bfloat16 [64, 4608, 16], P('mp'), may hold values from -0.09375 to 0.09375
- projected_lowrank_right: bfloat16 [64, 16, 3, 32, 128], P(None, None, None, 'mp'), as said below
- result_lowrank_left: bfloat16 [64, 4096, 16], P(None, 'mp'), may hold values from -0.09375 to 0.09375
- result_lowrank_right: bfloat16 [64, 16, 4608], P('mp'), may hold values from -1.5 to 1.5
- token_request: int32 [4, 512], P('dp'), may hold values from 0 to 7, never falling along the last dimension, each value on 1 to 256 neighbouring positions
- lowrank_choice_by_prompt: int32 [4, 8], P('dp'), may hold values from 0 to 63
- adapter_position: int32 [64], replicated, may hold values from 0 to 63, each once
- request_pages: int32 [4, 8, 4], replicated, may hold values from 0 to 255
Outputs:
- hidden_out: bfloat16 [2048, 4608], P(('dp', 'mp'))
- kv_new: bfloat16 [2048, 2, 32, 128], P('dp', None, 'mp')
Inputs may be any that keep to these rules, and one draw needn't show every extreme that they name: `key_value_weight`: query heads h and h2 with h // 2 == h2 // 2 have equal key and value weights: they share one key and value head. `key_value_cache`: query heads that share a key and value head have equal cached keys and values. `projected_lowrank_right`: the key and value parts of query heads that share a key and value head are equal. `token_request`: numbers never fall along a group; every request has at least one token. `adapter_position`: each slot once. `request_pages`: pages may repeat within and across requests.
All inputs are finite; a program needn't handle non-finite values.
Results may differ from a plain program's by a relative error of at most 0.035.
Values may be sent and summed in bfloat16 or wider, within the bound.
No kernel may reach another device: no remote copies, remote signals or barrier semaphores. Data moves between devices by JAX's collectives and lax.ppermute only.
A program may use at most 128 MiB of HBM per device.

v0:
```python
import math
import jax
import jax.numpy as jnp
from jax import lax
from jax.sharding import PartitionSpec as P

HIDDEN_BREADTH = 4608
ASKING_CHANNELS = 32
CHANNEL_LENGTH = 128
NUM_LOW_TERMS = 64
LOW_DIMENSION = 16
SHARD_PROMPTS = 8
PPR = 4
PAGE = 16
EPS = 1e-06
SOFTCAP = 50.0


def rms_scale(values, scaling):
    mean_square = jnp.mean(values * values, axis=-1, keepdims=True)
    return values * lax.rsqrt(mean_square + EPS) * scaling


def apply_rotary(values, token_positions):
    half_dim = values.shape[-1] // 2
    frequency = 10000.0 ** (-2.0 * jnp.arange(half_dim, dtype=jnp.float32) / values.shape[-1])
    angles = token_positions.astype(jnp.float32)[:, None] * frequency[None, :]
    cosine = jnp.cos(angles)[:, None, :]
    sine_part = jnp.sin(angles)[:, None, :]
    first_half = values[..., :half_dim]
    second_half = values[..., half_dim:]
    return jnp.concatenate(
        [
            first_half * cosine - second_half * sine_part,
            second_half * cosine + first_half * sine_part,
        ],
        axis=-1,
    )


def positions_of(segments):
    length = segments.shape[0]
    earlier = jnp.sum((segments[None, :] < segments[:, None]).astype(jnp.int32), axis=1)
    return PPR * PAGE + jnp.arange(length, dtype=jnp.int32) - earlier


def capped(scores):
    return SOFTCAP * jnp.tanh(scores / SOFTCAP)


def attend_local(query_rows, keys_new, fresh_values, keys_pre, values_pre, segments):
    scale_factor = 1.0 / math.sqrt(HIDDEN_BREADTH // ASKING_CHANNELS)
    length = segments.shape[0]
    prefix_owner = jnp.arange(keys_pre.shape[1], dtype=jnp.int32) // (PPR * PAGE)
    mask_pre = (prefix_owner[None, :] == segments[:, None])[None]
    ordinal = jnp.arange(length, dtype=jnp.int32)
    mask_new = ((segments[None, :] == segments[:, None]) & (ordinal[None, :] <= ordinal[:, None]))[
        None
    ]
    scores_pre = (
        jnp.einsum("thd,hjd->htj", query_rows, keys_pre, preferred_element_type=jnp.float32)
        * scale_factor
    )
    scores_new = (
        jnp.einsum("thd,uhd->htu", query_rows, keys_new, preferred_element_type=jnp.float32)
        * scale_factor
    )
    weight_pre = jnp.where(mask_pre, jnp.exp(capped(scores_pre)), 0.0)
    weight_new = jnp.where(mask_new, jnp.exp(capped(scores_new)), 0.0)
    totals = jnp.sum(weight_pre, axis=-1, keepdims=True) + jnp.sum(
        weight_new, axis=-1, keepdims=True
    )
    probs_pre = (weight_pre / totals).astype(jnp.bfloat16)
    probs_new = (weight_new / totals).astype(jnp.bfloat16)
    mixture = jnp.einsum("htj,hjd->thd", probs_pre, values_pre, preferred_element_type=jnp.float32)
    mixture = mixture + jnp.einsum(
        "htu,uhd->thd", probs_new, fresh_values, preferred_element_type=jnp.float32
    )
    return mixture.astype(jnp.bfloat16).reshape(length, -1)


def shards(
    residual_input,
    before_attention_gain,
    after_attention_gain,
    before_feedforward_gain,
    after_feedforward_gain,
    query_weight,
    key_value_weight,
    output_weight,
    gate_matrix,
    up_matrix,
    down_matrix,
    key_value_cache,
    projected_lowrank_left,
    projected_lowrank_right,
    result_lowrank_left,
    result_lowrank_right,
    token_request,
    lowrank_choice_by_prompt,
    adapter_position,
    request_pages,
):
    mp_index = lax.axis_index("mp")
    dp_index = lax.axis_index("dp")
    residual = residual_input.astype(jnp.float32)
    normed_rows = rms_scale(residual, before_attention_gain).astype(jnp.bfloat16)
    normalized_rows = lax.all_gather(normed_rows, "mp", axis=0, tiled=True)
    prompt_ordinal = normalized_rows.shape[0]
    channel_window = query_weight.shape[1] // CHANNEL_LENGTH
    query_rows = jnp.dot(normalized_rows, query_weight, preferred_element_type=jnp.float32).reshape(
        prompt_ordinal, channel_window, CHANNEL_LENGTH
    )
    key_value_rows = jnp.dot(
        normalized_rows,
        key_value_weight.reshape(HIDDEN_BREADTH, 2 * channel_window * CHANNEL_LENGTH),
        preferred_element_type=jnp.float32,
    ).reshape(prompt_ordinal, 2, channel_window, CHANNEL_LENGTH)
    segments = token_request[0]
    request_ids = lowrank_choice_by_prompt[0]
    request_range = jnp.arange(SHARD_PROMPTS, dtype=jnp.int32)
    membership = segments[:, None] == request_range[None, :]
    adapter_range = jnp.arange(NUM_LOW_TERMS, dtype=jnp.int32)
    token_adapter = jnp.sum(jnp.where(membership, request_ids[None, :], 0), axis=1)
    token_adapter_slot = jnp.sum(
        jnp.where(token_adapter[:, None] == adapter_range[None, :], adapter_position[None, :], 0),
        axis=1,
    )
    gathered_down = lax.all_gather(projected_lowrank_left, "mp", axis=0, tiled=True)
    request_slot = jnp.sum(
        jnp.where(request_ids[:, None] == adapter_range[None, :], adapter_position[None, :], 0),
        axis=1,
    )
    request_down = gathered_down[request_slot]
    request_factors = jnp.einsum(
        "td,rdk->trk", normalized_rows, request_down, preferred_element_type=jnp.float32
    )
    lowrank_source = jnp.sum(jnp.where(membership[:, :, None], request_factors, 0.0), axis=1)
    lowrank_source = lowrank_source.astype(jnp.bfloat16)
    choice_mask_table = membership.astype(jnp.bfloat16)
    broadened_lines = (choice_mask_table[:, :, None] * lowrank_source[:, None, :]).reshape(
        prompt_ordinal, SHARD_PROMPTS * LOW_DIMENSION
    )
    raised_result_lines = projected_lowrank_right[request_ids].reshape(
        SHARD_PROMPTS * LOW_DIMENSION, 3 * channel_window * CHANNEL_LENGTH
    )
    adapter_query_key_value = jnp.dot(
        broadened_lines, raised_result_lines, preferred_element_type=jnp.float32
    ).reshape(prompt_ordinal, 3, channel_window, CHANNEL_LENGTH)
    token_positions = positions_of(segments)
    rotary_queries = apply_rotary(
        query_rows + adapter_query_key_value[:, 0], token_positions
    ).astype(jnp.bfloat16)
    rotary_keys = apply_rotary(
        key_value_rows[:, 0] + adapter_query_key_value[:, 1], token_positions
    ).astype(jnp.bfloat16)
    fresh_values = (key_value_rows[:, 1] + adapter_query_key_value[:, 2]).astype(jnp.bfloat16)
    kv_new = jnp.stack([rotary_keys, fresh_values], axis=1)
    own_pages = lax.dynamic_index_in_dim(request_pages, dp_index, 0, keepdims=False).reshape(
        SHARD_PROMPTS * PPR
    )
    whole_pool = lax.all_gather(key_value_cache, "dp", axis=0, tiled=True)
    chosen = whole_pool[own_pages]
    keys_pre = jnp.transpose(chosen[:, 0], (1, 0, 2, 3)).reshape(
        channel_window, SHARD_PROMPTS * PPR * PAGE, CHANNEL_LENGTH
    )
    values_pre = jnp.transpose(chosen[:, 1], (1, 0, 2, 3)).reshape(
        channel_window, SHARD_PROMPTS * PPR * PAGE, CHANNEL_LENGTH
    )
    attended = attend_local(
        rotary_queries, rotary_keys, fresh_values, keys_pre, values_pre, segments
    )
    request_output_down = result_lowrank_left[request_ids]
    request_output_factors = jnp.einsum(
        "tc,rck->trk", attended, request_output_down, preferred_element_type=jnp.float32
    )
    output_adapter_piece = jnp.sum(
        jnp.where(membership[:, :, None], request_output_factors, 0.0), axis=1
    )
    result_lowrank_source = lax.psum(output_adapter_piece.astype(jnp.bfloat16), "mp")
    result_seat_lines = result_lowrank_right.shape[0]
    output_slots = mp_index * result_seat_lines + jnp.arange(result_seat_lines, dtype=jnp.int32)
    resident_here = (token_adapter_slot[:, None] == output_slots[None, :]).astype(jnp.bfloat16)
    broadened_result = (resident_here[:, :, None] * result_lowrank_source[:, None, :]).reshape(
        prompt_ordinal, result_seat_lines * LOW_DIMENSION
    )
    raised_window = result_lowrank_right.reshape(result_seat_lines * LOW_DIMENSION, HIDDEN_BREADTH)
    attn_sum = lax.psum_scatter(
        (
            jnp.dot(attended, output_weight, preferred_element_type=jnp.float32)
            + jnp.dot(broadened_result, raised_window, preferred_element_type=jnp.float32)
        ).astype(jnp.bfloat16),
        "mp",
        scatter_dimension=0,
        tiled=True,
    ).astype(jnp.float32)
    after_attn = (residual + rms_scale(attn_sum, after_attention_gain)).astype(jnp.bfloat16)
    normed_ffw = rms_scale(after_attn.astype(jnp.float32), before_feedforward_gain).astype(
        jnp.bfloat16
    )
    piece = lax.all_gather(normed_ffw, "mp", axis=0, tiled=True)
    gated = jnp.dot(piece, gate_matrix, preferred_element_type=jnp.float32)
    upward = jnp.dot(piece, up_matrix, preferred_element_type=jnp.float32)
    hidden = (jax.nn.gelu(gated, approximate=True) * upward).astype(jnp.bfloat16)
    ffw_sum = lax.psum_scatter(
        jnp.dot(hidden, down_matrix, preferred_element_type=jnp.float32).astype(jnp.bfloat16),
        "mp",
        scatter_dimension=0,
        tiled=True,
    ).astype(jnp.float32)
    hidden_out = (
        after_attn.astype(jnp.float32) + rms_scale(ffw_sum, after_feedforward_gain)
    ).astype(jnp.bfloat16)
    return (hidden_out, kv_new)


def solution(mesh):
    return jax.shard_map(
        shards,
        mesh=mesh,
        in_specs=(
            P(("dp", "mp"), None),
            P(),
            P(),
            P(),
            P(),
            P(None, "mp"),
            P(None, None, "mp", None),
            P("mp", None),
            P(None, "mp"),
            P(None, "mp"),
            P("mp", None),
            P("dp", None, "mp", None, None),
            P("mp", None, None),
            P(None, None, None, "mp", None),
            P(None, "mp", None),
            P("mp", None, None),
            P("dp", None),
            P("dp", None),
            P(),
            P(),
        ),
        out_specs=(P(("dp", "mp"), None), P("dp", None, "mp", None)),
        check_vma=False,
    )
```

profile of v0, /device:TPU:0, one launch (start us, length us, event | category | flops | bytes accessed | tf_op | source)
XLA Modules:
  0.0 1112.8 jit_solution(17951339612052338414)
XLA Ops:
  7.2 0.7 all-gather.5.cloned.1.call-update
  8.0 1.1 fusion.31
  9.0 1.7 fusion.33
  10.8 0.7 all-gather.9.cloned.1.call-update
  11.5 0.7 constant_dynamic-slice_fusion
  12.2 0.1 copy.46
  12.3 0.1 reshape.488
  12.4 0.7 fusion.73
  13.1 2.1 gather_fusion.3
  15.2 1.7 gather_fusion.2
  16.9 0.8 copy.48
  17.7 2.0 copy.60
  19.7 2.5 copy.50
  22.3 0.2 select_reduce_fusion.4
  22.5 0.1 select_reduce_fusion.3
  22.6 0.1 select_reduce_fusion.2
  22.7 0.2 convert_reduce_fusion
  23.0 15.9 %all-gather.5.cloned.1.call-done = bf16[256,2,1,16,128]{4,3,2,1,0:T(8,128)(2,1)} async-done(((bf16[64,2,1,16,128]{4,3,2,1,0:T(8,128)(2,1)}), bf16[256,2,1,16,128]{4,3,2,1,0:T(8,128)(2,1)}) %all-gather.5.cloned.1.call-update) | async-done | bytes 2097168 | tf_op jit(solution)/shard_map/all_gather | solution.py:162
  38.9 2.2 gather_fusion
  41.2 157.9 %all-gather.7.cloned.1.call-done = bf16[512,4608]{1,0:T(8,128)(2,1)} async-done(((bf16[16,4608]{1,0:T(8,128)(2,1)}), bf16[512,4608]{1,0:T(8,128)(2,1)}) %all-gather.7.cloned.1.call-update) | async-done | bytes 4718608 | tf_op jit(solution)/shard_map/all_gather | solution.py:108
  199.1 4.5 fusion.19
  203.6 207.7 %all-gather.9.cloned.1.call-done = bf16[64,4608,16]{1,2,0:T(8,128)(2,1)} async-done(((bf16[2,4608,16]{1,2,0:T(8,128)(2,1)}), bf16[64,4608,16]{1,2,0:T(8,128)(2,1)}) %all-gather.9.cloned.1.call-update) | async-done | bytes 9437200 | tf_op jit(solution)/shard_map/all_gather | solution.py:129
  411.2 4.3 gather_fusion.1
  415.6 4.1 fusion.84
  419.8 0.2 convolution_bitcast_fusion
  420.0 0.1 fusion.39
  420.1 1.7 fusion.22
  421.8 0.6 fusion.54
  422.4 0.5 fusion.82
  422.9 0.5 fusion.83
  423.4 0.3 fusion.26
  423.7 0.2 fusion.24
  423.9 0.2 fusion.86
  424.2 157.2 %psum.7 = bf16[512,16]{0,1:T(8,128)(2,1)S(1)} all-reduce(bf16[512,16]{0,1:T(8,128)(2,1)S(1)} %select_reduce_fusion), channel_id=1, replica_groups=mesh['dp'=4,'mp'=32] {'mp'}, use_global_device_ids=true, to_apply=%region_9.10 | all-reduce | flops 8192 | bytes 32768 | tf_op jit(solution)/shard_map/psum | solution.py:180
  581.4 1.4 fusion.63
  582.8 3.5 fusion
  586.4 165.2 %reduce-scatter.3.cloned.1.call-done = bf16[16,4608]{1,0:T(8,128)(2,1)} async-done(((bf16[512,4608]{1,0:T(8,128)(2,1)}), bf16[16,4608]{1,0:T(8,128)(2,1)}) %reduce-scatter.3.cloned.1.call-update) | async-done | bytes 147472 | tf_op jit(solution)/shard_map/reduce_scatter | solution.py:188
  751.6 1.1 fusion.27
  752.7 1.2 fusion.35
  753.9 0.8 fusion.37
  754.7 0.2 reduce-scatter.5.cloned.1.call-start
  754.9 154.9 %all-gather.11.cloned.1.call-done = bf16[512,4608]{1,0:T(8,128)(2,1)} async-done(((bf16[16,4608]{1,0:T(8,128)(2,1)}), bf16[512,4608]{1,0:T(8,128)(2,1)}) %all-gather.11.cloned.1.call-update) | async-done | bytes 4718608 | tf_op jit(solution)/shard_map/all_gather | solution.py:201
  909.8 7.4 fusion.85
  917.2 14.2 %convolution_convert_fusion = bf16[512,4608]{1,0:T(8,128)(2,1)} fusion(bf16[640,4608]{1,0:T(8,128)(2,1)} %param.30, bf16[512,4608]{1,0:T(8,128)(2,1)} %all-gather.11.cloned.1.call-done, bf16[4608,640]{1,0:T(8,128)(2,1)} %param.29, f32[512,640]{1,0:T(8,128)S(1)} %fusion.85), kind=kOutput, calls=%fused_computation.6 | convolution fusion | flops 6045433856 | bytes 22544384 | tf_op jit(solution)/shard_map/dot_general | solution.py:206
  931.5 0.9 copy.52
  932.4 170.8 %reduce-scatter.5.cloned.1.call-done = bf16[16,4608]{1,0:T(8,128)(2,1)} async-done(((bf16[512,4608]{1,0:T(8,128)(2,1)}), bf16[16,4608]{1,0:T(8,128)(2,1)}) %reduce-scatter.5.cloned.1.call-update) | async-done | bytes 147472 | tf_op jit(solution)/shard_map/reduce_scatter | solution.py:205
  1103.2 1.1 fusion.29
  1104.3 1.7 fusion.38
  (63 shorter events, 0.7 us)
Async XLA Ops:
  7.2 575.7 %copy-start = (bf16[128,4608]{1,0:T(8,128)(2,1)S(1)}, bf16[128,4608]{1,0:T(8,128)(2,1)}, u32[]{:S(2)}) copy-start(bf16[128,4608]{1,0:T(8,128)(2,1)} %param.27) | copy-start | bytes 3538948
  7.2 31.8 %all-gather.5.cloned.1.call-start = ((), (), s32[]{:S(2)}) async-start(), calls=%async_computation.2 | async-start | bytes 2621440 | tf_op jit(solution)/shard_map/all_gather | solution.py:162
  7.9 191.1 %all-gather.7.cloned.1.call-start = ((), (), s32[]{:S(2)}) async-start(), calls=%async_computation.3 | async-start | bytes 4866048 | tf_op jit(solution)/shard_map/all_gather | solution.py:108
  10.7 400.5 %all-gather.9.cloned.1.call-start = ((), (), s32[]{:S(2)}) async-start(), calls=%async_computation.4 | async-start | bytes 9732096 | tf_op jit(solution)/shard_map/all_gather | solution.py:129
  11.5 740.1 %reduce-scatter.3.cloned.1.call-start = ((), (), s32[]{:S(2)}) async-start(), calls=%async_computation.5 | async-start | bytes 4866048 | tf_op jit(solution)/shard_map/reduce_scatter | solution.py:188
  17.7 4.6 copy-start.11
  17.7 4.6 copy-start.12
  17.7 4.8 copy-start.7
  415.5 4.2 copy-start.5
  415.5 4.6 slice-start
  415.6 4.6 copy-start.4
  415.6 4.6 slice-start.1
  422.9 1.0 copy-start.2
  423.4 158.0 %copy-start.6 = (bf16[2,16,4608]{2,1,0:T(8,128)(2,1)S(1)}, bf16[2,16,4608]{2,1,0:T(8,128)(2,1)}, u32[]{:S(2)}) copy-start(bf16[2,16,4608]{2,1,0:T(8,128)(2,1)} %param.35) | copy-start | bytes 884740
  586.4 166.3 %copy-start.3 = (bf16[16,4608]{1,0:T(8,128)(2,1)S(1)}, bf16[16,4608]{1,0:T(8,128)(2,1)}, u32[]{:S(2)}) copy-start(bf16[16,4608]{1,0:T(8,128)(2,1)} %param.20) | copy-start | bytes 442372
  586.4 166.3 %copy-start.8 = (f32[4608]{0:T(1024)S(1)}, f32[4608]{0:T(1024)}, u32[]{:S(2)}) copy-start(f32[4608]{0:T(1024)} %param.22) | copy-start | bytes 55300
  586.4 167.5 %copy-start.9 = (f32[4608]{0:T(1024)S(1)}, f32[4608]{0:T(1024)}, u32[]{:S(2)}) copy-start(f32[4608]{0:T(1024)} %param.23) | copy-start | bytes 55300
  586.4 323.4 %all-gather.11.cloned.1.call-start = ((), (), s32[]{:S(2)}) async-start(), calls=%async_computation.6 | async-start | bytes 4866048 | tf_op jit(solution)/shard_map/all_gather | solution.py:201
  754.7 348.5 %reduce-scatter.5.cloned.1.call-start = ((), (), s32[]{:S(2)}) async-start(), calls=%async_computation.7 | async-start | bytes 4866048 | tf_op jit(solution)/shard_map/reduce_scatter | solution.py:205
  917.2 188.7 %copy-start.1 = (bf16[128,4608]{1,0:T(8,128)(2,1)S(1)}, bf16[128,4608]{1,0:T(8,128)(2,1)}, u32[]{:S(2)}) copy-start(bf16[128,4608]{1,0:T(8,128)(2,1)} %param.27) | copy-start | bytes 3538948
  931.5 172.8 %copy-start.10 = (f32[4608]{0:T(1024)S(1)}, f32[4608]{0:T(1024)}, u32[]{:S(2)}) copy-start(f32[4608]{0:T(1024)} %param.24) | copy-start | bytes 55300
Sparse Core Ops, SparseCore 0:
  9.7 29.2 all-gather.4
  41.1 157.8 all-gather.6
  200.7 210.4 all-gather.8
  586.5 165.0 reduce-scatter.2
  754.8 154.9 all-gather.10
  931.6 171.5 reduce-scatter.4
where the time goes:
time: 1110 us
  waiting for transfers between devices  874 us (79%)
  blocking collectives  157 us (14%)
  matrix products  38.8 us (3%)
  local copies, waits for them, and re-layouts  17.5 us (2%)
  between operations  14.5 us (1%)
    all_gather x1, waiting for transfers between devices, shards(): lax.all_gather(projected_lowrank_left, 'mp', axis=0, tiled=True)  208 us
    reduce_scatter x1, waiting for transfers between devices, shards(): lax.psum_scatter(jnp.dot(hidden, down_matrix, preferred_element_type=jnp....  171 us
    reduce_scatter x1, waiting for transfers between devices, shards(): lax.psum_scatter((jnp.dot(attended, output_weight, preferred_element_type...  165 us
    all_gather x1, waiting for transfers between devices, shards(): normalized_rows = lax.all_gather(normed_rows, 'mp', axis=0, tiled=True)  158 us
    psum x1, blocking collectives, shards(): lax.psum(output_adapter_piece.astype(jnp.bfloat16), 'mp')  157 us
    all_gather x1, waiting for transfers between devices, shards(): piece = lax.all_gather(normed_ffw, 'mp', axis=0, tiled=True)  155 us
  transfers between devices with their start and end apart: 6, of which 6 were waited for; matrix products, arithmetic and copies ran while one was open for 2% of the time, Pallas kernels for 0%

commit v1 on v0

--- a/solution.py
+++ b/solution.py
@@ -177,7 +177,9 @@
     output_adapter_piece = jnp.sum(
         jnp.where(membership[:, :, None], request_output_factors, 0.0), axis=1
     )
-    result_lowrank_source = lax.psum(output_adapter_piece.astype(jnp.bfloat16), "mp")
+    result_lowrank_source = jnp.sum(
+        lax.all_gather(output_adapter_piece.astype(jnp.bfloat16), "mp"), axis=0
+    )
     result_seat_lines = result_lowrank_right.shape[0]
     output_slots = mp_index * result_seat_lines + jnp.arange(result_seat_lines, dtype=jnp.int32)
     resident_here = (token_adapter_slot[:, None] == output_slots[None, :]).astype(jnp.bfloat16)

time: 1110 us -> 1040 us (0.937)
  blocking collectives: 157 us -> 83.4 us
    psum x1 -> x0, blocking collectives: 157 us -> none  [shards(): lax.psum(output_adapter_piece.astype(jnp.bfloat16), 'mp')]
    all_gather x0 -> x1, blocking collectives: none -> 83.4 us  [shards(): lax.all_gather(output_adapter_piece.astype(jnp.bfloat16), 'mp')]
where the time goes in v1:
time: 1040 us
  waiting for transfers between devices  873 us (84%)
  blocking collectives  83.4 us (8%)
  matrix products  38.8 us (4%)
  local copies, waits for them, and re-layouts  17.6 us (2%)
  between operations  14.5 us (1%)
  other arithmetic  10.8 us (1%)
    all_gather x1, waiting for transfers between devices, shards(): lax.all_gather(projected_lowrank_left, 'mp', axis=0, tiled=True)  208 us
    reduce_scatter x1, waiting for transfers between devices, shards(): lax.psum_scatter(jnp.dot(hidden, down_matrix, preferred_element_type=jnp....  171 us
    reduce_scatter x1, waiting for transfers between devices, shards(): lax.psum_scatter((jnp.dot(attended, output_weight, preferred_element_type...  165 us
    all_gather x1, waiting for transfers between devices, shards(): normalized_rows = lax.all_gather(normed_rows, 'mp', axis=0, tiled=True)  158 us
    all_gather x1, waiting for transfers between devices, shards(): piece = lax.all_gather(normed_ffw, 'mp', axis=0, tiled=True)  154 us
    all_gather x1, blocking collectives, shards(): lax.all_gather(output_adapter_piece.astype(jnp.bfloat16), 'mp')  83.4 us
  transfers between devices with their start and end apart: 6, of which 6 were waited for; matrix products, arithmetic and copies ran while one was open for 2% of the time, Pallas kernels for 0%

profile of v1, /device:TPU:0, one launch (start us, length us, event | category | flops | bytes accessed | tf_op | source)
XLA Modules:
  0.0 1038.3 jit_solution(6048571489283260224)
XLA Ops:
  7.2 0.7 all-gather.6.cloned.1.call-update
  8.0 1.1 fusion.31
  9.0 1.7 fusion.33
  10.8 0.7 all-gather.10.cloned.1.call-update
  11.5 0.7 constant_dynamic-slice_fusion
  12.4 0.7 fusion.73
  13.1 2.1 gather_fusion.3
  15.2 1.7 gather_fusion.2
  16.9 0.8 copy.50
  17.7 2.0 copy.63
  19.7 2.5 copy.52
  22.3 0.2 select_reduce_fusion.4
  22.5 0.1 select_reduce_fusion.3
  22.6 0.1 select_reduce_fusion.2
  22.7 0.2 convert_reduce_fusion
  23.0 15.9 %all-gather.6.cloned.1.call-done = bf16[256,2,1,16,128]{4,3,2,1,0:T(8,128)(2,1)} async-done(((bf16[64,2,1,16,128]{4,3,2,1,0:T(8,128)(2,1)}), bf16[256,2,1,16,128]{4,3,2,1,0:T(8,128)(2,1)}) %all-gather.6.cloned.1.call-update) | async-done | bytes 2097168 | tf_op jit(solution)/shard_map/all_gather | solution.py:162
  38.9 2.2 gather_fusion
  41.2 157.9 %all-gather.8.cloned.1.call-done = bf16[512,4608]{1,0:T(8,128)(2,1)} async-done(((bf16[16,4608]{1,0:T(8,128)(2,1)}), bf16[512,4608]{1,0:T(8,128)(2,1)}) %all-gather.8.cloned.1.call-update) | async-done | bytes 4718608 | tf_op jit(solution)/shard_map/all_gather | solution.py:108
  199.1 4.5 fusion.19
  203.6 207.7 %all-gather.10.cloned.1.call-done = bf16[64,4608,16]{1,2,0:T(8,128)(2,1)} async-done(((bf16[2,4608,16]{1,2,0:T(8,128)(2,1)}), bf16[64,4608,16]{1,2,0:T(8,128)(2,1)}) %all-gather.10.cloned.1.call-update) | async-done | bytes 9437200 | tf_op jit(solution)/shard_map/all_gather | solution.py:129
  411.2 4.3 gather_fusion.1
  415.6 4.1 fusion.84
  419.8 0.2 convolution_bitcast_fusion
  420.0 0.1 fusion.39
  420.1 1.7 fusion.22
  421.8 0.6 fusion.54
  422.4 0.5 fusion.82
  422.9 0.5 fusion.83
  423.4 0.3 fusion.26
  423.7 0.2 fusion.24
  423.9 0.2 fusion.86
  424.2 83.4 %all-gather = bf16[16384,16]{0,1:T(8,128)(2,1)S(1)} all-gather(bf16[512,16]{0,1:T(8,128)(2,1)S(1)} %select_reduce_fusion), channel_id=2, replica_groups=mesh['dp'=4,'mp'=32] {'mp'}, dimensions={0}, use_global_device_ids=true | all-gather | bytes 540672 | tf_op jit(solution)/shard_map/all_gather | solution.py:181
  507.5 0.2 copy.60
  507.7 0.2 bitcast_reduce_fusion
  507.8 1.4 fusion.63
  509.3 3.5 fusion
  512.9 165.3 %reduce-scatter.3.cloned.1.call-done = bf16[16,4608]{1,0:T(8,128)(2,1)} async-done(((bf16[512,4608]{1,0:T(8,128)(2,1)}), bf16[16,4608]{1,0:T(8,128)(2,1)}) %reduce-scatter.3.cloned.1.call-update) | async-done | bytes 147472 | tf_op jit(solution)/shard_map/reduce_scatter | solution.py:190
  678.2 1.1 fusion.27
  679.3 1.2 fusion.35
  680.4 0.8 fusion.37
  681.2 0.2 reduce-scatter.5.cloned.1.call-start
  681.5 154.0 %all-gather.12.cloned.1.call-done = bf16[512,4608]{1,0:T(8,128)(2,1)} async-done(((bf16[16,4608]{1,0:T(8,128)(2,1)}), bf16[512,4608]{1,0:T(8,128)(2,1)}) %all-gather.12.cloned.1.call-update) | async-done | bytes 4718608 | tf_op jit(solution)/shard_map/all_gather | solution.py:203
  835.4 7.4 fusion.85
  842.9 14.2 %convolution_convert_fusion = bf16[512,4608]{1,0:T(8,128)(2,1)} fusion(bf16[640,4608]{1,0:T(8,128)(2,1)} %param.30, bf16[512,4608]{1,0:T(8,128)(2,1)} %all-gather.12.cloned.1.call-done, bf16[4608,640]{1,0:T(8,128)(2,1)} %param.29, f32[512,640]{1,0:T(8,128)S(1)} %fusion.85), kind=kOutput, calls=%fused_computation.6 | convolution fusion | flops 6045433856 | bytes 22544384 | tf_op jit(solution)/shard_map/dot_general | solution.py:208
  857.1 0.9 copy.54
  858.0 170.6 %reduce-scatter.5.cloned.1.call-done = bf16[16,4608]{1,0:T(8,128)(2,1)} async-done(((bf16[512,4608]{1,0:T(8,128)(2,1)}), bf16[16,4608]{1,0:T(8,128)(2,1)}) %reduce-scatter.5.cloned.1.call-update) | async-done | bytes 147472 | tf_op jit(solution)/shard_map/reduce_scatter | solution.py:207
  1028.7 1.1 fusion.29
  1029.7 1.7 fusion.38
  (65 shorter events, 0.9 us)
Async XLA Ops:
  7.2 502.1 %copy-start = (bf16[128,4608]{1,0:T(8,128)(2,1)S(1)}, bf16[128,4608]{1,0:T(8,128)(2,1)}, u32[]{:S(2)}) copy-start(bf16[128,4608]{1,0:T(8,128)(2,1)} %param.27) | copy-start | bytes 3538948
  7.2 31.8 %all-gather.6.cloned.1.call-start = ((), (), s32[]{:S(2)}) async-start(), calls=%async_computation.2 | async-start | bytes 2621440 | tf_op jit(solution)/shard_map/all_gather | solution.py:162
  7.9 191.1 %all-gather.8.cloned.1.call-start = ((), (), s32[]{:S(2)}) async-start(), calls=%async_computation.3 | async-start | bytes 4866048 | tf_op jit(solution)/shard_map/all_gather | solution.py:108
  10.7 400.5 %all-gather.10.cloned.1.call-start = ((), (), s32[]{:S(2)}) async-start(), calls=%async_computation.4 | async-start | bytes 9732096 | tf_op jit(solution)/shard_map/all_gather | solution.py:129
  11.5 666.7 %reduce-scatter.3.cloned.1.call-start = ((), (), s32[]{:S(2)}) async-start(), calls=%async_computation.5 | async-start | bytes 4866048 | tf_op jit(solution)/shard_map/reduce_scatter | solution.py:190
  17.7 4.6 copy-start.11
  17.7 4.6 copy-start.12
  17.7 4.8 copy-start.7
  415.5 4.2 copy-start.5
  415.5 4.6 slice-start
  415.6 4.6 copy-start.4
  415.6 4.6 slice-start.1
  422.9 1.0 copy-start.2
  423.4 84.4 %copy-start.6 = (bf16[2,16,4608]{2,1,0:T(8,128)(2,1)S(1)}, bf16[2,16,4608]{2,1,0:T(8,128)(2,1)}, u32[]{:S(2)}) copy-start(bf16[2,16,4608]{2,1,0:T(8,128)(2,1)} %param.35) | copy-start | bytes 884740
  512.8 166.4 %copy-start.3 = (bf16[16,4608]{1,0:T(8,128)(2,1)S(1)}, bf16[16,4608]{1,0:T(8,128)(2,1)}, u32[]{:S(2)}) copy-start(bf16[16,4608]{1,0:T(8,128)(2,1)} %param.20) | copy-start | bytes 442372
  512.8 166.4 %copy-start.8 = (f32[4608]{0:T(1024)S(1)}, f32[4608]{0:T(1024)}, u32[]{:S(2)}) copy-start(f32[4608]{0:T(1024)} %param.22) | copy-start | bytes 55300
  512.8 167.6 %copy-start.9 = (f32[4608]{0:T(1024)S(1)}, f32[4608]{0:T(1024)}, u32[]{:S(2)}) copy-start(f32[4608]{0:T(1024)} %param.23) | copy-start | bytes 55300
  512.8 322.6 %all-gather.12.cloned.1.call-start = ((), (), s32[]{:S(2)}) async-start(), calls=%async_computation.6 | async-start | bytes 4866048 | tf_op jit(solution)/shard_map/all_gather | solution.py:203
  681.2 347.4 %reduce-scatter.5.cloned.1.call-start = ((), (), s32[]{:S(2)}) async-start(), calls=%async_computation.7 | async-start | bytes 4866048 | tf_op jit(solution)/shard_map/reduce_scatter | solution.py:207
  842.8 188.6 %copy-start.1 = (bf16[128,4608]{1,0:T(8,128)(2,1)S(1)}, bf16[128,4608]{1,0:T(8,128)(2,1)}, u32[]{:S(2)}) copy-start(bf16[128,4608]{1,0:T(8,128)(2,1)} %param.27) | copy-start | bytes 3538948
  857.1 172.6 %copy-start.10 = (f32[4608]{0:T(1024)S(1)}, f32[4608]{0:T(1024)}, u32[]{:S(2)}) copy-start(f32[4608]{0:T(1024)} %param.24) | copy-start | bytes 55300
Sparse Core Ops, SparseCore 0:
  9.7 29.2 all-gather.5
  41.1 157.8 all-gather.7
  200.7 210.4 all-gather.9
  513.0 165.1 reduce-scatter.2
  681.3 154.0 all-gather.11
  857.2 171.3 reduce-scatter.4
